TPU v7x, 512 devices: a whole 4x8x8 slice. The times are simulated.
512 devices in a mesh: seq: 128 (over z, y, core), head: 4 (over x).
Axes of the slice: x: 4, y: 8, z: 8, core: 2. Of those that a mesh axis runs over, the one named last changes fastest.
Arguments:
- tokens: bfloat16 [16384, 4096], P('seq', 'head'), may hold values from -120 to 120
- shared_weight: bfloat16 [4096, 512], P(None, 'head'), may hold values from -0.75 to 0.75
- value_weight: bfloat16 [4096, 512], P(None, 'head'), may hold values from -0.09375 to 0.09375
- head_grad: bfloat16 [16384, 512], P('seq', 'head'), may hold values from -0.75 to 0.75
- sorted_slot: int32 [4, 16384], P('head', 'seq'), may hold values from 0 to 16383, as said below
Outputs:
- shared_grad: float32 [4096, 512], P('seq', 'head')
- value_grad: float32 [4096, 512], P('seq', 'head')
Inputs may be any that keep to these rules, and one draw needn't show every extreme that they name: For each head, sorted_slot[h] is a permutation of the positions. Of the 128 positions of one device (positions r * 128 to (r+1) * 128 - 1), at most 2 have sorted indices in the range s * 128 to (s+1) * 128 - 1 of one device s, for every head, and in every head some pair r, s reaches 2.
All inputs are finite; a program needn't handle non-finite values.
Results may differ from a plain program's by a relative error of at most 0.006.
The roundings to bfloat16 on the way count: a program that leaves them out, or rounds other values in their place, can miss the bound.
Values may be sent and summed in bfloat16 or wider, within the bound.
No kernel may reach another device: no remote copies, remote signals or barrier semaphores. Data moves between devices by JAX's collectives and lax.ppermute only.
A program may use at most 64 MiB of HBM per device.

v0:
```python
import math
import jax
import jax.numpy as jnp
from jax import lax
from jax.sharding import Mesh
from jax.sharding import PartitionSpec as P

GROUP = 64
SEQ = ("z", "y", "c")
eps_norm = 1e-06
masked_score = -1000000000.0


def shifted(value, axis, steps):
    count = lax.axis_size(axis)
    pairs = [(source, (source + steps) % count) for source in range(count)]
    return lax.ppermute(value, axis, pairs)


def unit_keys(block):
    block_float = block.astype(jnp.float32)
    norm_rows = jnp.sqrt(jnp.sum(block_float * block_float, axis=1, keepdims=True) + eps_norm)
    return (block_float / norm_rows).astype(jnp.bfloat16)


def per_device(tokens, shared_weight, value_weight, head_grad, sorted_slot):
    whole = lax.all_gather(tokens, "head", axis=1, tiled=True)
    tok_count = whole.shape[0]
    feat_count = whole.shape[1]
    head_width = shared_weight.shape[1]
    peer_count = lax.axis_size(SEQ)
    capacity = 2 * tok_count // peer_count
    group_count = tok_count // GROUP
    tail_start = tok_count - GROUP
    scale_factor = 1.0 / math.sqrt(head_width)
    query = jnp.dot(whole, shared_weight, preferred_element_type=jnp.float32).astype(jnp.bfloat16)
    values = jnp.dot(whole, value_weight, preferred_element_type=jnp.float32).astype(jnp.bfloat16)
    slot_ids = sorted_slot[0]
    target = slot_ids // tok_count
    local_slot = slot_ids - target * tok_count
    peer_ids = jnp.arange(peer_count, dtype=jnp.int32)
    row_ids = jnp.arange(tok_count, dtype=jnp.int32)
    earlier_rows = (row_ids[:, None] > row_ids[None, :]).astype(jnp.bfloat16)
    every_row = jnp.ones((tok_count,), dtype=bool)
    one_hot = ((target[:, None] == peer_ids[None, :]) & every_row[:, None]).astype(jnp.bfloat16)
    before = jnp.dot(earlier_rows, one_hot, preferred_element_type=jnp.float32)
    buffer_index = target * capacity + jnp.sum(before * one_hot.astype(jnp.float32), axis=1).astype(
        jnp.int32
    )
    payload = jnp.concatenate([query, values, head_grad], axis=1)
    send_rows = (
        jnp.zeros((peer_count * capacity, 3 * head_width), jnp.bfloat16)
        .at[buffer_index]
        .set(payload)
    )
    send_slots = (
        jnp.full((peer_count * capacity,), tok_count, jnp.int32).at[buffer_index].set(local_slot)
    )
    recv_rows, recv_slots = (
        lax.all_to_all(send_rows, SEQ, split_axis=0, concat_axis=0, tiled=True),
        lax.all_to_all(send_slots, SEQ, split_axis=0, concat_axis=0, tiled=True),
    )
    sorted_rows = (
        jnp.zeros((tok_count, 3 * head_width), jnp.bfloat16)
        .at[recv_slots]
        .set(recv_rows, mode="drop")
    )
    halo_rows = shifted(sorted_rows[tail_start:, : 2 * head_width], SEQ, 1)
    sorted_query = sorted_rows[:, :head_width]
    own_keys = unit_keys(sorted_query).reshape(group_count, GROUP, head_width)
    halo_keys = unit_keys(halo_rows[:, :head_width])
    q_blocks = sorted_query.reshape(group_count, GROUP, head_width)
    v_blocks = sorted_rows[:, head_width : 2 * head_width].reshape(group_count, GROUP, head_width)
    g_blocks = sorted_rows[:, 2 * head_width :].reshape(group_count, GROUP, head_width)
    prev_keys = jnp.concatenate([halo_keys[None], own_keys[:-1]], axis=0)
    prev_values = jnp.concatenate([halo_rows[None, :, head_width:], v_blocks[:-1]], axis=0)
    key_window = jnp.concatenate([own_keys, prev_keys], axis=1)
    value_window = jnp.concatenate([v_blocks, prev_values], axis=1)
    scores = (
        jnp.einsum("cqd,ckd->cqk", q_blocks, key_window, preferred_element_type=jnp.float32)
        * scale_factor
    )
    self_mask = jnp.arange(GROUP)[:, None] == jnp.arange(2 * GROUP)[None, :]
    scores = jnp.where(self_mask[None], masked_score, scores)
    probs = jax.nn.softmax(scores, axis=-1)
    dprob = jnp.einsum("cqd,ckd->cqk", g_blocks, value_window, preferred_element_type=jnp.float32)
    dscore = probs * (dprob - jnp.sum(probs * dprob, axis=-1, keepdims=True))
    probs_low = probs.astype(jnp.bfloat16)
    dscore_low = dscore.astype(jnp.bfloat16)
    dquery = (
        jnp.einsum("cqk,ckd->cqd", dscore_low, key_window, preferred_element_type=jnp.float32)
        * scale_factor
    )
    dkey_window = (
        jnp.einsum("cqk,cqd->ckd", dscore_low, q_blocks, preferred_element_type=jnp.float32)
        * scale_factor
    )
    dvalue_window = jnp.einsum(
        "cqk,cqd->ckd", probs_low, g_blocks, preferred_element_type=jnp.float32
    )
    grad_window = jnp.concatenate([dkey_window, dvalue_window], axis=-1)
    own_part = grad_window[:, :GROUP]
    later_part = grad_window[1:, GROUP:]
    outgoing = grad_window[0, GROUP:]
    incoming = shifted(outgoing, SEQ, -1)
    key_value = (own_part + jnp.concatenate([later_part, incoming[None]], axis=0)).reshape(
        tok_count, 2 * head_width
    )
    dquery_s = dquery.reshape(tok_count, head_width)
    dkey_s = key_value[:, :head_width]
    dvalue_s = key_value[:, head_width:]
    query_float = sorted_query.astype(jnp.float32)
    norm_s = jnp.sqrt(jnp.sum(query_float * query_float, axis=1, keepdims=True) + eps_norm)
    along = jnp.sum(query_float * dkey_s, axis=1, keepdims=True)
    dshared_s = dquery_s + dkey_s / norm_s - query_float * (along / norm_s**3)
    sorted_grads = jnp.concatenate(
        [dshared_s.astype(jnp.bfloat16), dvalue_s.astype(jnp.bfloat16)], axis=1
    )
    return_rows = sorted_grads[jnp.minimum(recv_slots, tok_count - 1)]
    back_rows = lax.all_to_all(return_rows, SEQ, split_axis=0, concat_axis=0, tiled=True)
    combined = back_rows[buffer_index]
    nz, ny, nc = (lax.axis_size(a) for a in SEQ)
    blocks = whole.reshape(tok_count, nz, ny, nc, feat_count // (nz * ny * nc))
    partial = jnp.einsum(
        "pzyck,ph->cyzkh", blocks, combined, preferred_element_type=jnp.float32
    ).reshape(feat_count, 2 * head_width)
    grads = partial
    for axis in ("c", "y", "z"):
        grads = lax.psum_scatter(grads, axis, scatter_dimension=0, tiled=True)
    return (grads[:, :head_width], grads[:, head_width:])


def split_mesh(mesh):
    devices = mesh.devices
    seq_n, head_n = devices.shape
    column = devices[:, 0]
    cores = sorted({d.core_on_chip for d in column})
    ys = sorted({d.coords[1] for d in column})
    nc, ny = (len(cores), len(ys))
    nz = seq_n // (nc * ny)
    grid = devices.reshape(nz, ny, nc, head_n)
    for z in range(nz):
        for y in range(ny):
            for c in range(nc):
                d = grid[z, y, c, 0]
                assert d.core_on_chip == cores[c] and d.coords[1] == ys[y]
    return Mesh(grid, SEQ + ("head",))


def solution(mesh):
    fine = split_mesh(mesh)
    in_specs = (P(SEQ, "head"), P(None, "head"), P(None, "head"), P(SEQ, "head"), P("head", SEQ))
    out_specs = (P(SEQ, "head"), P(SEQ, "head"))
    return jax.shard_map(
        per_device, mesh=fine, in_specs=in_specs, out_specs=out_specs, check_vma=False
    )
```

profile of v0, /device:TPU:2, one launch (start us, length us, event | category | flops | bytes accessed | tf_op | source)
XLA Modules:
  0.0 232.9 jit_solution(7353964962916671930)
XLA Ops:
  7.2 0.0 copy-start
  7.2 0.0 all-gather.2.cloned.1.call-start
  7.2 0.7 all-gather.2.cloned.1.call-update
  7.9 0.7 bitcast_subtract_fusion
  8.6 0.2 fusion.4
  8.8 0.7 fusion.32
  9.4 1.0 scatter_custom_fusion
  10.4 0.8 all_to_all.24
  11.2 17.8 %all-to-all-start = ((s32[128,2,1]{1,2,0:T(1,128)}), s32[128,2,1]{1,2,0:T(1,128)S(1)}, u32[]{:S(2)}, u32[]{:S(2)}) async-start(s32[128,2,1]{1,2,0:T(1,128)} %bitcast.4), calls=%async_computation | async-start | bytes 131072 | tf_op jit(solution)/shard_map/all_to_all | solution.py:61
  29.0 0.9 copy.16
  29.9 12.8 %all-gather.2.cloned.1.call-done = bf16[128,4096]{1,0:T(8,128)(2,1)} async-done(((bf16[128,1024]{1,0:T(8,128)(2,1)}), bf16[128,4096]{1,0:T(8,128)(2,1)}) %all-gather.2.cloned.1.call-update) | async-done | bytes 1048592 | tf_op jit(solution)/shard_map/all_gather | solution.py:27
  42.7 0.0 copy-done
  42.7 1.7 convolution_convert_fusion
  44.4 2.1 convolution_convert_fusion.1
  46.5 0.1 copy.17
  46.6 1.1 scatter_custom_fusion.1
  47.8 0.0 copy-start.1
  47.8 0.8 all_to_all.27
  48.5 0.0 all-to-all-done
  48.5 14.9 %all-to-all-start.1 = ((bf16[128,2,384]{2,1,0:T(2,128)(2,1)}), bf16[128,2,384]{2,1,0:T(2,128)(2,1)S(1)}, u32[]{:S(2)}, u32[]{:S(2)}) async-start(bf16[128,2,384]{2,1,0:T(2,128)(2,1)} %all_to_all.27), calls=%async_computation.1 | async-start | bytes 393216 | tf_op jit(solution)/shard_map/all_to_all | solution.py:60
  63.4 0.5 broadcast.207
  63.9 0.8 reduce.3
  64.7 0.1 all_to_all.26
  64.9 11.9 %all-to-all-done.1 = bf16[128,2,384]{2,1,0:T(2,128)(2,1)S(1)} async-done(((bf16[128,2,384]{2,1,0:T(2,128)(2,1)}), bf16[128,2,384]{2,1,0:T(2,128)(2,1)S(1)}, u32[]{:S(2)}, u32[]{:S(2)}) %all-to-all-start.1) | async-done | bytes 196640 | tf_op jit(solution)/shard_map/all_to_all | solution.py:60
  76.9 0.1 reshape.266
  76.9 1.5 scatter_custom_fusion.2
  78.4 0.1 fusion.11
  78.6 0.1 fusion.12
  78.7 2.0 collective-permute-start
  80.7 6.5 %collective-permute-done = bf16[64,256]{1,0:T(8,128)(2,1)S(1)} collective-permute-done((bf16[64,256]{1,0:T(8,128)(2,1)S(1)}, bf16[64,256]{1,0:T(8,128)(2,1)S(1)}, u32[]{:S(2)}, u32[]{:S(2)}) %collective-permute-start) | collective-permute-done | bytes 32800 | tf_op jit(solution)/shard_map/ppermute | solution.py:17
  87.3 0.1 fusion.25
  87.4 0.1 fusion.30
  87.5 0.3 fusion.45
  87.8 0.4 fusion.27
  88.2 0.3 multiply_reduce_fusion
  88.5 0.1 multiply_convert_fusion
  88.6 0.2 convolution_multiply_fusion
  88.8 0.1 fusion.7
  88.9 1.9 collective-permute-start.1
  90.9 0.1 convolution_multiply_fusion.1
  91.0 2.4 %collective-permute-done.1 = f32[64,256]{0,1:T(8,128)S(1)} collective-permute-done((f32[64,256]{0,1:T(8,128)S(1)}, f32[64,256]{0,1:T(8,128)S(1)}, u32[]{:S(2)}, u32[]{:S(2)}) %collective-permute-start.1) | collective-permute-done | bytes 65568 | tf_op jit(solution)/shard_map/ppermute | solution.py:17
  93.4 0.1 copy.18
  93.5 0.1 fusion.13
  93.7 0.1 fusion.15
  93.8 1.2 gather_fusion
  94.9 0.7 all_to_all.30
  95.7 8.7 %all-to-all-start.2 = ((bf16[128,2,256]{2,1,0:T(2,128)(2,1)}), bf16[128,2,256]{2,1,0:T(2,128)(2,1)S(1)}, u32[]{:S(2)}, u32[]{:S(2)}) async-start(bf16[128,2,256]{2,1,0:T(2,128)(2,1)} %all_to_all.30), calls=%async_computation.2 | async-start | bytes 262144 | tf_op jit(solution)/shard_map/all_to_all | solution.py:120
  104.4 0.0 reduce-scatter.4.cloned.1.call-start
  104.4 12.1 %all-to-all-done.2 = bf16[128,2,256]{2,1,0:T(2,128)(2,1)S(1)} async-done(((bf16[128,2,256]{2,1,0:T(2,128)(2,1)}), bf16[128,2,256]{2,1,0:T(2,128)(2,1)S(1)}, u32[]{:S(2)}, u32[]{:S(2)}) %all-to-all-start.2) | async-done | bytes 131104 | tf_op jit(solution)/shard_map/all_to_all | solution.py:120
  116.6 0.1 all_to_all.32
  116.6 0.8 gather_fusion.1
  117.5 0.0 copy-done.1
  117.5 0.7 fusion.46
  118.2 2.2 copy.20
  120.5 0.0 reduce-scatter.4.cloned.1.call-update
  120.5 0.0 reduce-scatter.6.cloned.1.call-start
  120.5 12.8 %reduce-scatter.4.cloned.1.call-done = f32[2048,256]{1,0:T(8,128)} async-done(((f32[4096,256]{1,0:T(8,128)}), f32[2048,256]{1,0:T(8,128)}) %reduce-scatter.4.cloned.1.call-update) | async-done | bytes 2097168 | tf_op jit(solution)/shard_map/reduce_scatter | solution.py:129
  133.4 0.0 reduce-scatter.6.cloned.1.call-update
  133.4 0.0 reduce-scatter.8.cloned.1.call-start
  133.4 49.3 %reduce-scatter.6.cloned.1.call-done = f32[256,256]{1,0:T(8,128)} async-done(((f32[2048,256]{1,0:T(8,128)}), f32[256,256]{1,0:T(8,128)}) %reduce-scatter.6.cloned.1.call-update) | async-done | bytes 262160 | tf_op jit(solution)/shard_map/reduce_scatter | solution.py:129
  182.7 0.0 reduce-scatter.8.cloned.1.call-update
  182.8 42.2 %reduce-scatter.8.cloned.1.call-done = f32[32,256]{1,0:T(8,128)} async-done(((f32[256,256]{1,0:T(8,128)}), f32[32,256]{1,0:T(8,128)}) %reduce-scatter.8.cloned.1.call-update) | async-done | bytes 32784 | tf_op jit(solution)/shard_map/reduce_scatter | solution.py:129
  225.0 1.3 fusion.44
  (16 shorter events, 0.1 us)
Async XLA Ops:
  7.2 35.5 %copy-start = (bf16[4096,128]{1,0:T(8,128)(2,1)S(1)}, bf16[4096,128]{1,0:T(8,128)(2,1)}, u32[]{:S(2)}) copy-start(bf16[4096,128]{1,0:T(8,128)(2,1)} %param.7) | copy-start | bytes 3145732
  7.2 35.5 %all-gather.2.cloned.1.call-start = ((), (), s32[]{:S(2)}) async-start(), calls=%async_computation.6 | async-start | bytes 1310720 | tf_op jit(solution)/shard_map/all_gather | solution.py:27
  11.2 37.4 %all-to-all-start = ((s32[128,2,1]{1,2,0:T(1,128)}), s32[128,2,1]{1,2,0:T(1,128)S(1)}, u32[]{:S(2)}, u32[]{:S(2)}) async-start(s32[128,2,1]{1,2,0:T(1,128)} %bitcast.4), calls=%async_computation | async-start | bytes 131072 | tf_op jit(solution)/shard_map/all_to_all | solution.py:61
  47.8 69.7 %copy-start.1 = (bf16[128,4096]{1,0:T(8,128)(2,1)S(1)}, bf16[128,4096]{1,0:T(8,128)(2,1)}, u32[]{:S(2)}) copy-start(bf16[128,4096]{1,0:T(8,128)(2,1)} %all-gather.2.cloned.1.call-done) | copy-start | bytes 3145732
  48.5 28.3 %all-to-all-start.1 = ((bf16[128,2,384]{2,1,0:T(2,128)(2,1)}), bf16[128,2,384]{2,1,0:T(2,128)(2,1)S(1)}, u32[]{:S(2)}, u32[]{:S(2)}) async-start(bf16[128,2,384]{2,1,0:T(2,128)(2,1)} %all_to_all.27), calls=%async_computation.1 | async-start | bytes 393216 | tf_op jit(solution)/shard_map/all_to_all | solution.py:60
  78.7 8.6 %collective-permute-start = (bf16[64,256]{1,0:T(8,128)(2,1)S(1)}, bf16[64,256]{1,0:T(8,128)(2,1)S(1)}, u32[]{:S(2)}, u32[]{:S(2)}) collective-permute-start(bf16[64,256]{1,0:T(8,128)(2,1)S(1)} %slice.75), channel_id=1, source_target_pairs={{0,4},{4,8},{8,12},{12,16},{16,20},{20,24},{24,28},{28,32},{32,36}... | collective-permute-start | bytes 98312 | tf_op jit(solution)/shard_map/ppermute | solution.py:17
  88.9 4.4 %collective-permute-start.1 = (f32[64,256]{0,1:T(8,128)S(1)}, f32[64,256]{0,1:T(8,128)S(1)}, u32[]{:S(2)}, u32[]{:S(2)}) collective-permute-start(f32[64,256]{0,1:T(8,128)S(1)} %get-tuple-element.5), channel_id=1, source_target_pairs={{0,508},{4,0},{8,4},{12,8},{16,12},{20,16},{24,20},{28,24},{32,28}... | collective-permute-start | bytes 196616 | tf_op jit(solution)/shard_map/ppermute | solution.py:17
  95.7 20.9 %all-to-all-start.2 = ((bf16[128,2,256]{2,1,0:T(2,128)(2,1)}), bf16[128,2,256]{2,1,0:T(2,128)(2,1)S(1)}, u32[]{:S(2)}, u32[]{:S(2)}) async-start(bf16[128,2,256]{2,1,0:T(2,128)(2,1)} %all_to_all.30), calls=%async_computation.2 | async-start | bytes 262144 | tf_op jit(solution)/shard_map/all_to_all | solution.py:120
  104.4 29.0 %reduce-scatter.4.cloned.1.call-start = ((), (), s32[]{:S(2)}) async-start(), calls=%async_computation.7 | async-start | bytes 6291456 | tf_op jit(solution)/shard_map/reduce_scatter | solution.py:129
  120.5 62.2 %reduce-scatter.6.cloned.1.call-start = ((), (), s32[]{:S(2)}) async-start(), calls=%async_computation.8 | async-start | bytes 2359296 | tf_op jit(solution)/shard_map/reduce_scatter | solution.py:129
  133.4 91.6 %reduce-scatter.8.cloned.1.call-start = ((), (), s32[]{:S(2)}) async-start(), calls=%async_computation.9 | async-start | bytes 294912 | tf_op jit(solution)/shard_map/reduce_scatter | solution.py:129
Sparse Core Ops, SparseCore 0:
  10.1 32.5 all-gather.1
  120.6 12.7 reduce-scatter.3
  136.2 46.4 reduce-scatter.5
  185.4 39.5 reduce-scatter.7
where the time goes:
time: 233 us
  waiting for transfers between devices  151 us (65%)
  starting transfers between devices  45.5 us (20%)
  between operations  14.1 us (6%)
  local copies, waits for them, and re-layouts  13.3 us (6%)
  matrix products  6.05 us (3%)
  other arithmetic  3.1 us (1%)
    reduce_scatter x3, waiting for transfers between devices, per_device(): grads = lax.psum_scatter(grads, axis, scatter_dimension=0, tiled=True)  104 us
    all_to_all x1, starting transfers between devices, per_device(): lax.all_to_all(send_slots, SEQ, split_axis=0, concat_axis=0, tiled=True)  17.8 us
    all_to_all x1, starting transfers between devices, per_device(): lax.all_to_all(send_rows, SEQ, split_axis=0, concat_axis=0, tiled=True)  14.9 us
    all_gather x1, waiting for transfers between devices, per_device(): whole = lax.all_gather(tokens, 'head', axis=1, tiled=True)  12.8 us
    all_to_all x1, waiting for transfers between devices, per_device(): lax.all_to_all(return_rows, SEQ, split_axis=0, concat_axis=0, tiled=True)  12.1 us
    all_to_all x1, waiting for transfers between devices, per_device(): lax.all_to_all(send_rows, SEQ, split_axis=0, concat_axis=0, tiled=True)  11.9 us
    ppermute x2, waiting for transfers between devices, shifted(): return lax.ppermute(value, axis, pairs)  8.87 us
    all_to_all x1, starting transfers between devices, per_device(): lax.all_to_all(return_rows, SEQ, split_axis=0, concat_axis=0, tiled=True)  8.7 us
  transfers between devices with their start and end apart: 9, of which 8 were waited for; matrix products, arithmetic and copies ran while one was open for 4% of the time, Pallas kernels for 0%

commit v1 on v0

--- a/solution.py
+++ b/solution.py
@@ -24,7 +24,9 @@
 
 
 def per_device(tokens, shared_weight, value_weight, head_grad, sorted_slot):
-    whole = lax.all_gather(tokens, "head", axis=1, tiled=True)
+    whole = jnp.concatenate(
+        lax.all_to_all(jnp.stack([tokens] * lax.axis_size("head")), "head", 0, 0), axis=1
+    )
     tok_count = whole.shape[0]
     feat_count = whole.shape[1]
     head_width = shared_weight.shape[1]

time: 233 us -> 232 us (level)
  matrix products: 6.05 us -> 3.16 us
  local copies, waits for them, and re-layouts: 13.3 us -> 15.7 us
    all_gather x1 -> x0, waiting for transfers between devices: 12.8 us -> none  [per_device(): whole = lax.all_gather(tokens, 'head', axis=1, tiled=True)]
    all_to_all x0 -> x1, starting transfers between devices: none -> 9.36 us  [per_device(): lax.all_to_all(jnp.stack([tokens] * lax.axis_size('head')), 'head', 0, 0)]
    all_to_all x1, starting transfers between devices: 14.9 us -> 6.17 us  [per_device(): lax.all_to_all(send_rows, SEQ, split_axis=0, concat_axis=0, tiled=True)]
    all_to_all x1, waiting for transfers between devices: 0.01 us -> 8.17 us  [per_device(): lax.all_to_all(send_slots, SEQ, split_axis=0, concat_axis=0, tiled=True)]
    all_to_all x0 -> x1, waiting for transfers between devices: none -> 5.3 us  [per_device(): lax.all_to_all(jnp.stack([tokens] * lax.axis_size('head')), 'head', 0, 0)]
  transfers between devices with their start and end apart: 9 -> 9, of which waited for: 8 -> 9; matrix products, arithmetic and copies ran while one was open for 4% -> 3% of each run, Pallas kernels for 0% -> 0%
where the time goes in v1:
time: 232 us
  waiting for transfers between devices  150 us (65%)
  starting transfers between devices  45.8 us (20%)
  local copies, waits for them, and re-layouts  15.7 us (7%)
  between operations  14.1 us (6%)
  matrix products  3.16 us (1%)
  other arithmetic  3.11 us (1%)
    reduce_scatter x3, waiting for transfers between devices, per_device(): grads = lax.psum_scatter(grads, axis, scatter_dimension=0, tiled=True)  103 us
    all_to_all x1, starting transfers between devices, per_device(): lax.all_to_all(send_slots, SEQ, split_axis=0, concat_axis=0, tiled=True)  17.5 us
    all_to_all x1, waiting for transfers between devices, per_device(): lax.all_to_all(return_rows, SEQ, split_axis=0, concat_axis=0, tiled=True)  12.1 us
    all_to_all x1, waiting for transfers between devices, per_device(): lax.all_to_all(send_rows, SEQ, split_axis=0, concat_axis=0, tiled=True)  11.9 us
    all_to_all x1, starting transfers between devices, per_device(): lax.all_to_all(jnp.stack([tokens] * lax.axis_size('head')), 'head', 0, 0)  9.36 us
    ppermute x2, waiting for transfers between devices, shifted(): return lax.ppermute(value, axis, pairs)  8.87 us
    all_to_all x1, starting transfers between devices, per_device(): lax.all_to_all(return_rows, SEQ, split_axis=0, concat_axis=0, tiled=True)  8.7 us
    all_to_all x1, waiting for transfers between devices, per_device(): lax.all_to_all(send_slots, SEQ, split_axis=0, concat_axis=0, tiled=True)  8.17 us
  transfers between devices with their start and end apart: 9, of which 9 were waited for; matrix products, arithmetic and copies ran while one was open for 3% of the time, Pallas kernels for 0%

profile of v1, /device:TPU:2, one launch (start us, length us, event | category | flops | bytes accessed | tf_op | source)
XLA Modules:
  0.0 231.7 jit_solution(4067041207606551499)
XLA Ops:
  7.2 0.0 copy-start
  7.2 0.0 copy-start.1
  7.2 1.3 copy.16
  8.5 1.1 stack.2
  9.6 9.4 %all-to-all-start.1 = ((bf16[4,128,1024]{1,2,0:T(8,128)(2,1)}), bf16[4,128,1024]{1,2,0:T(8,128)(2,1)S(1)}, u32[]{:S(2)}, u32[]{:S(2)}) async-start(bf16[4,128,1024]{1,2,0:T(8,128)(2,1)} %stack.2), calls=%async_computation.1 | async-start | bytes 2097152 | tf_op jit(solution)/shard_map/all_to_all | solution.py:28
  19.0 0.9 copy.17
  19.8 0.7 bitcast_subtract_fusion
  20.5 0.2 fusion.4
  20.7 0.7 fusion.32
  21.3 1.0 scatter_custom_fusion
  22.3 0.8 all_to_all.27
  23.1 5.3 %all-to-all-done.1 = bf16[4,128,1024]{1,2,0:T(8,128)(2,1)S(1)} async-done(((bf16[4,128,1024]{1,2,0:T(8,128)(2,1)}), bf16[4,128,1024]{1,2,0:T(8,128)(2,1)S(1)}, u32[]{:S(2)}, u32[]{:S(2)}) %all-to-all-start.1) | async-done | bytes 1048608 | tf_op jit(solution)/shard_map/all_to_all | solution.py:28
  28.4 17.5 %all-to-all-start = ((s32[128,2,1]{1,2,0:T(1,128)}), s32[128,2,1]{1,2,0:T(1,128)S(1)}, u32[]{:S(2)}, u32[]{:S(2)}) async-start(s32[128,2,1]{1,2,0:T(1,128)} %bitcast.4), calls=%async_computation | async-start | bytes 131072 | tf_op jit(solution)/shard_map/all_to_all | solution.py:63
  45.9 0.0 copy-done
  45.9 0.5 convolution_convert_fusion
  46.4 0.0 copy-done.1
  46.4 0.5 convolution_convert_fusion.1
  46.9 0.1 copy.18
  47.0 1.1 scatter_custom_fusion.1
  48.1 0.7 all_to_all.31
  48.9 8.2 %all-to-all-done = s32[128,2,1]{1,2,0:T(1,128)S(1)} async-done(((s32[128,2,1]{1,2,0:T(1,128)}), s32[128,2,1]{1,2,0:T(1,128)S(1)}, u32[]{:S(2)}, u32[]{:S(2)}) %all-to-all-start) | async-done | bytes 1056 | tf_op jit(solution)/shard_map/all_to_all | solution.py:63
  57.0 6.2 %all-to-all-start.2 = ((bf16[128,2,384]{2,1,0:T(2,128)(2,1)}), bf16[128,2,384]{2,1,0:T(2,128)(2,1)S(1)}, u32[]{:S(2)}, u32[]{:S(2)}) async-start(bf16[128,2,384]{2,1,0:T(2,128)(2,1)} %all_to_all.31), calls=%async_computation.2 | async-start | bytes 393216 | tf_op jit(solution)/shard_map/all_to_all | solution.py:62
  63.2 0.5 broadcast.209
  63.7 0.8 reduce.3
  64.6 0.1 all_to_all.29
  64.7 11.9 %all-to-all-done.2 = bf16[128,2,384]{2,1,0:T(2,128)(2,1)S(1)} async-done(((bf16[128,2,384]{2,1,0:T(2,128)(2,1)}), bf16[128,2,384]{2,1,0:T(2,128)(2,1)S(1)}, u32[]{:S(2)}, u32[]{:S(2)}) %all-to-all-start.2) | async-done | bytes 196640 | tf_op jit(solution)/shard_map/all_to_all | solution.py:62
  76.7 0.1 reshape.272
  76.8 1.5 scatter_custom_fusion.2
  78.2 0.1 fusion.11
  78.4 0.1 fusion.12
  78.5 2.0 collective-permute-start
  80.6 6.5 %collective-permute-done = bf16[64,256]{1,0:T(8,128)(2,1)S(1)} collective-permute-done((bf16[64,256]{1,0:T(8,128)(2,1)S(1)}, bf16[64,256]{1,0:T(8,128)(2,1)S(1)}, u32[]{:S(2)}, u32[]{:S(2)}) %collective-permute-start) | collective-permute-done | bytes 32800 | tf_op jit(solution)/shard_map/ppermute | solution.py:17
  87.1 0.1 fusion.25
  87.2 0.1 fusion.30
  87.3 0.3 fusion.45
  87.6 0.4 fusion.27
  88.0 0.3 multiply_reduce_fusion
  88.3 0.1 multiply_convert_fusion
  88.4 0.2 convolution_multiply_fusion
  88.6 0.1 fusion.7
  88.8 1.9 collective-permute-start.1
  90.7 0.1 convolution_multiply_fusion.1
  90.8 2.4 %collective-permute-done.1 = f32[64,256]{0,1:T(8,128)S(1)} collective-permute-done((f32[64,256]{0,1:T(8,128)S(1)}, f32[64,256]{0,1:T(8,128)S(1)}, u32[]{:S(2)}, u32[]{:S(2)}) %collective-permute-start.1) | collective-permute-done | bytes 65568 | tf_op jit(solution)/shard_map/ppermute | solution.py:17
  93.2 0.1 copy.19
  93.3 0.1 fusion.13
  93.5 0.1 fusion.15
  93.6 1.2 gather_fusion
  94.8 0.7 all_to_all.34
  95.5 8.7 %all-to-all-start.3 = ((bf16[128,2,256]{2,1,0:T(2,128)(2,1)}), bf16[128,2,256]{2,1,0:T(2,128)(2,1)S(1)}, u32[]{:S(2)}, u32[]{:S(2)}) async-start(bf16[128,2,256]{2,1,0:T(2,128)(2,1)} %all_to_all.34), calls=%async_computation.3 | async-start | bytes 262144 | tf_op jit(solution)/shard_map/all_to_all | solution.py:122
  104.2 0.0 reduce-scatter.4.cloned.1.call-start
  104.2 12.1 %all-to-all-done.3 = bf16[128,2,256]{2,1,0:T(2,128)(2,1)S(1)} async-done(((bf16[128,2,256]{2,1,0:T(2,128)(2,1)}), bf16[128,2,256]{2,1,0:T(2,128)(2,1)S(1)}, u32[]{:S(2)}, u32[]{:S(2)}) %all-to-all-start.3) | async-done | bytes 131104 | tf_op jit(solution)/shard_map/all_to_all | solution.py:122
  116.4 0.1 all_to_all.36
  116.4 0.8 gather_fusion.1
  117.3 0.7 fusion.46
  118.0 2.2 copy.20
  120.2 0.0 reduce-scatter.4.cloned.1.call-update
  120.3 0.0 reduce-scatter.6.cloned.1.call-start
  120.3 11.6 %reduce-scatter.4.cloned.1.call-done = f32[2048,256]{1,0:T(8,128)} async-done(((f32[4096,256]{1,0:T(8,128)}), f32[2048,256]{1,0:T(8,128)}) %reduce-scatter.4.cloned.1.call-update) | async-done | bytes 2097168 | tf_op jit(solution)/shard_map/reduce_scatter | solution.py:131
  131.9 0.0 reduce-scatter.6.cloned.1.call-update
  132.0 0.0 reduce-scatter.8.cloned.1.call-start
  132.0 49.2 %reduce-scatter.6.cloned.1.call-done = f32[256,256]{1,0:T(8,128)} async-done(((f32[2048,256]{1,0:T(8,128)}), f32[256,256]{1,0:T(8,128)}) %reduce-scatter.6.cloned.1.call-update) | async-done | bytes 262160 | tf_op jit(solution)/shard_map/reduce_scatter | solution.py:131
  181.2 0.0 reduce-scatter.8.cloned.1.call-update
  181.3 42.6 %reduce-scatter.8.cloned.1.call-done = f32[32,256]{1,0:T(8,128)} async-done(((f32[256,256]{1,0:T(8,128)}), f32[32,256]{1,0:T(8,128)}) %reduce-scatter.8.cloned.1.call-update) | async-done | bytes 32784 | tf_op jit(solution)/shard_map/reduce_scatter | solution.py:131
  223.8 1.3 fusion.44
  (16 shorter events, 0.1 us)
Async XLA Ops:
  7.2 38.7 %copy-start = (bf16[4096,128]{1,0:T(8,128)(2,1)S(1)}, bf16[4096,128]{1,0:T(8,128)(2,1)}, u32[]{:S(2)}) copy-start(bf16[4096,128]{1,0:T(8,128)(2,1)} %param.7) | copy-start | bytes 3145732
  7.2 39.2 %copy-start.1 = (bf16[4096,128]{1,0:T(8,128)(2,1)S(1)}, bf16[4096,128]{1,0:T(8,128)(2,1)}, u32[]{:S(2)}) copy-start(bf16[4096,128]{1,0:T(8,128)(2,1)} %param.6) | copy-start | bytes 3145732
  9.6 18.8 %all-to-all-start.1 = ((bf16[4,128,1024]{1,2,0:T(8,128)(2,1)}), bf16[4,128,1024]{1,2,0:T(8,128)(2,1)S(1)}, u32[]{:S(2)}, u32[]{:S(2)}) async-start(bf16[4,128,1024]{1,2,0:T(8,128)(2,1)} %stack.2), calls=%async_computation.1 | async-start | bytes 2097152 | tf_op jit(solution)/shard_map/all_to_all | solution.py:28
  28.4 28.6 %all-to-all-start = ((s32[128,2,1]{1,2,0:T(1,128)}), s32[128,2,1]{1,2,0:T(1,128)S(1)}, u32[]{:S(2)}, u32[]{:S(2)}) async-start(s32[128,2,1]{1,2,0:T(1,128)} %bitcast.4), calls=%async_computation | async-start | bytes 131072 | tf_op jit(solution)/shard_map/all_to_all | solution.py:63
  57.0 19.6 %all-to-all-start.2 = ((bf16[128,2,384]{2,1,0:T(2,128)(2,1)}), bf16[128,2,384]{2,1,0:T(2,128)(2,1)S(1)}, u32[]{:S(2)}, u32[]{:S(2)}) async-start(bf16[128,2,384]{2,1,0:T(2,128)(2,1)} %all_to_all.31), calls=%async_computation.2 | async-start | bytes 393216 | tf_op jit(solution)/shard_map/all_to_all | solution.py:62
  78.5 8.6 %collective-permute-start = (bf16[64,256]{1,0:T(8,128)(2,1)S(1)}, bf16[64,256]{1,0:T(8,128)(2,1)S(1)}, u32[]{:S(2)}, u32[]{:S(2)}) collective-permute-start(bf16[64,256]{1,0:T(8,128)(2,1)S(1)} %slice.75), channel_id=1, source_target_pairs={{0,4},{4,8},{8,12},{12,16},{16,20},{20,24},{24,28},{28,32},{32,36}... | collective-permute-start | bytes 98312 | tf_op jit(solution)/shard_map/ppermute | solution.py:17
  88.8 4.4 %collective-permute-start.1 = (f32[64,256]{0,1:T(8,128)S(1)}, f32[64,256]{0,1:T(8,128)S(1)}, u32[]{:S(2)}, u32[]{:S(2)}) collective-permute-start(f32[64,256]{0,1:T(8,128)S(1)} %get-tuple-element.5), channel_id=1, source_target_pairs={{0,508},{4,0},{8,4},{12,8},{16,12},{20,16},{24,20},{28,24},{32,28}... | collective-permute-start | bytes 196616 | tf_op jit(solution)/shard_map/ppermute | solution.py:17
  95.5 20.9 %all-to-all-start.3 = ((bf16[128,2,256]{2,1,0:T(2,128)(2,1)}), bf16[128,2,256]{2,1,0:T(2,128)(2,1)S(1)}, u32[]{:S(2)}, u32[]{:S(2)}) async-start(bf16[128,2,256]{2,1,0:T(2,128)(2,1)} %all_to_all.34), calls=%async_computation.3 | async-start | bytes 262144 | tf_op jit(solution)/shard_map/all_to_all | solution.py:122
  104.2 27.8 %reduce-scatter.4.cloned.1.call-start = ((), (), s32[]{:S(2)}) async-start(), calls=%async_computation.7 | async-start | bytes 6291456 | tf_op jit(solution)/shard_map/reduce_scatter | solution.py:131
  120.3 61.0 %reduce-scatter.6.cloned.1.call-start = ((), (), s32[]{:S(2)}) async-start(), calls=%async_computation.8 | async-start | bytes 2359296 | tf_op jit(solution)/shard_map/reduce_scatter | solution.py:131
  132.0 91.9 %reduce-scatter.8.cloned.1.call-start = ((), (), s32[]{:S(2)}) async-start(), calls=%async_computation.9 | async-start | bytes 294912 | tf_op jit(solution)/shard_map/reduce_scatter | solution.py:131
Sparse Core Ops, SparseCore 0:
  120.4 11.5 reduce-scatter.3
  134.8 46.4 reduce-scatter.5
  184.0 39.7 reduce-scatter.7
